TPU v7x, 32 devices: a whole 2x2x4 slice. The times are simulated.
32 devices in a mesh: tile: 8 (over z, core), deg: 4 (over y, x).
Axes of the slice: x: 2, y: 2, z: 4, core: 2. Of those that a mesh axis runs over, the one named last changes fastest.
Arguments:
- field: float32 [3, 8, 128, 512], P(None, None, 'tile', 'deg'), may hold values from -6 to 6
- flow: float32 [3, 8, 128, 512], P(None, None, 'tile', 'deg'), may hold values from -3 to 3
- match_ops: bfloat16 [32, 512, 512], P(('tile', 'deg')), may hold values from -0.5 to 20.5
- wave_of_slot: int32 [32], replicated, may hold values from 0 to 31, each once
Outputs:
- advanced: float32 [3, 8, 128, 512], P(None, None, 'tile', 'deg')
Inputs may be any that keep to these rules, and one draw needn't show every extreme that they name: `wave_of_slot`: every wavenumber from 0 to 31 is named by exactly one slot.
All inputs are finite; a program needn't handle non-finite values.
Results may differ from a plain program's by a relative error of at most 0.00065.
Values may be sent and summed in bfloat16 or wider, within the bound.
No kernel may reach another device: no remote copies, remote signals or barrier semaphores. Data moves between devices by JAX's collectives and lax.ppermute only.
A program may use at most 64 MiB of HBM per device.

v0:
```python
import math
import jax
import jax.numpy as jnp
from jax import lax
from jax.sharding import PartitionSpec as P

P_SIZE = 8
diffusivity = 0.05
time_step = 0.01
highest = lax.Precision.HIGHEST
gll_interior = [0.2092992179024789, 0.5917001814331423, 0.8717401485096066]


def padded_2(value, sides, width):
    for axis, dim in sides:
        size, length = (lax.axis_size(axis), value.shape[dim])
        up = [(i, (i + 1) % size) for i in range(size)]
        down = [(j, i) for i, j in up]
        last = lax.slice_in_dim(value, length - width, length, axis=dim)
        first = lax.slice_in_dim(value, 0, width, axis=dim)
        before = lax.ppermute(last, axis, up)
        after = lax.ppermute(first, axis, down)
        value = jnp.concatenate([before, value, after], axis=dim)
    return value


def legendre_value(point, degree):
    previous = 1.0
    current = point
    for order in range(1, degree):
        following = ((2 * order + 1) * point * current - order * previous) / (order + 1)
        previous = current
        current = following
    return current


def gll_tables(count):
    degree = count - 1
    points = [-1.0] + [-value for value in reversed(gll_interior)] + list(gll_interior) + [1.0]
    values = [legendre_value(point, degree) for point in points]
    weights = [2.0 / (degree * (degree + 1) * value * value) for value in values]
    matrix = [
        [
            values[row] / (values[col] * (points[row] - points[col])) if row != col else 0.0
            for col in range(count)
        ]
        for row in range(count)
    ]
    matrix[0][0] = -degree * (degree + 1) / 4.0
    matrix[count - 1][count - 1] = degree * (degree + 1) / 4.0
    return (points, weights, matrix)


def apply_along(values, axis_pos, matrix):
    shape = values.shape
    blocks = values.reshape(
        shape[:axis_pos] + (shape[axis_pos] // P_SIZE, P_SIZE) + shape[axis_pos + 1 :]
    )
    letters = list("abcdefg"[: blocks.ndim])
    source = list(letters)
    source[axis_pos + 1] = "p"
    target = list(letters)
    target[axis_pos + 1] = "q"
    formula = "".join(source) + ",qp->" + "".join(target)
    return jnp.einsum(formula, blocks, matrix, precision=highest).reshape(shape)


def assemble_dim(values, axis_pos, left, right):
    shape = values.shape
    count = shape[axis_pos] // P_SIZE
    blocks = values.reshape(shape[:axis_pos] + (count, P_SIZE) + shape[axis_pos + 1 :])
    edge_shape = shape[:axis_pos] + (1, 1) + shape[axis_pos + 1 :]
    first = lax.slice_in_dim(blocks, 0, 1, axis=axis_pos + 1)
    last = lax.slice_in_dim(blocks, P_SIZE - 1, P_SIZE, axis=axis_pos + 1)
    before = jnp.concatenate(
        [left.reshape(edge_shape), lax.slice_in_dim(last, 0, count - 1, axis=axis_pos)],
        axis=axis_pos,
    )
    after = jnp.concatenate(
        [lax.slice_in_dim(first, 1, count, axis=axis_pos), right.reshape(edge_shape)], axis=axis_pos
    )
    middle = lax.slice_in_dim(blocks, 1, P_SIZE - 1, axis=axis_pos + 1)
    joined = jnp.concatenate([first + before, middle, last + after], axis=axis_pos + 1)
    return joined.reshape(shape)


def assembled_weights(weights, count, lead, trail):
    position = jnp.arange(count * P_SIZE, dtype=jnp.int32)
    local_point = position % P_SIZE
    element = position // P_SIZE
    base = jnp.tile(weights, count)
    starts = (
        jnp.where(local_point == 0, jnp.where(element > 0, 1.0, lead), 0.0) * weights[P_SIZE - 1]
    )
    ends = (
        jnp.where(local_point == P_SIZE - 1, jnp.where(element < count - 1, 1.0, trail), 0.0)
        * weights[0]
    )
    return base + starts + ends


def phases(waves, elem_start, elem_count, span, points):
    element = elem_start + jnp.arange(elem_count * P_SIZE, dtype=jnp.int32) // P_SIZE
    whole = waves[:, None] * (2 * element + 1)[None, :] % span
    fraction = waves.astype(jnp.float32)[:, None] * jnp.tile(points, elem_count)[None, :]
    return 2.0 * math.pi / span * (whole.astype(jnp.float32) + fraction)


def local(field, flow, match_ops, wave_of_slot):
    tiles = lax.axis_size("tile")
    groups = lax.axis_size("deg")
    tile_index = lax.axis_index("tile")
    group_index = lax.axis_index("deg")
    radial_nodes = field.shape[1]
    na_dev = field.shape[2]
    nb_dev = field.shape[3]
    elems_a = na_dev // P_SIZE
    elems_b = nb_dev // P_SIZE
    span = 2 * elems_a * tiles
    per_tile = wave_of_slot.shape[0] // tiles
    scale = P_SIZE / (na_dev * tiles)
    points_list, weights_list, matrix_list = gll_tables(P_SIZE)
    points = jnp.asarray(points_list, jnp.float32)
    weights = jnp.asarray(weights_list, jnp.float32)
    dmat = jnp.asarray(matrix_list, jnp.float32)
    block = jnp.kron(jnp.eye(elems_b, dtype=jnp.float32), dmat)
    lead = (group_index > 0).astype(jnp.float32)
    trail = (group_index < groups - 1).astype(jnp.float32)
    w_r = jnp.tile(weights, radial_nodes // P_SIZE)
    w_a = jnp.tile(weights, elems_a)
    w_b = jnp.tile(weights, elems_b)
    mass3 = w_r[:, None, None] * w_a[None, :, None] * w_b[None, None, :]
    surface_weight = w_a[:, None] * w_b[None, :]
    assembled = (
        assembled_weights(weights, radial_nodes // P_SIZE, 0.0, 0.0)[:, None, None]
        * assembled_weights(weights, elems_a, 1.0, 1.0)[None, :, None]
        * assembled_weights(weights, elems_b, lead, trail)[None, None, :]
    )
    column_mask = jnp.concatenate([lead[None], jnp.ones((nb_dev,), jnp.float32), trail[None]])

    def derive(values, direction, transpose):
        if direction == 2:
            table = block if transpose else block.T
            return jnp.dot(values, table, precision=highest)
        return apply_along(values, direction, dmat.T if transpose else dmat)

    flow_parts = [flow[0], flow[1], flow[2]]
    grad_flow = [
        [derive(flow_parts[component], direction, False) for direction in range(3)]
        for component in range(3)
    ]

    def analyse(surface):
        angle = phases(wave_of_slot, tile_index * elems_a, elems_a, span, points)
        table = (
            jnp.stack([jnp.cos(angle), jnp.sin(angle)], axis=1) * (w_a * scale)[None, None, :]
        ).reshape(lax.axis_size("tile") * per_tile * 2, na_dev)
        return jnp.dot(table, surface, precision=highest).reshape(
            lax.axis_size("tile") * per_tile, 2, nb_dev
        )

    def surface_flux(surface):
        coeff = lax.psum_scatter(analyse(surface), "tile", scatter_dimension=0, tiled=True)
        owned = lax.all_to_all(
            coeff.astype(jnp.bfloat16), "deg", split_axis=0, concat_axis=2, tiled=True
        )
        mapped = jnp.einsum("kpq,kcq->kcp", match_ops, owned, preferred_element_type=jnp.float32)
        matched = lax.all_to_all(mapped, "deg", split_axis=2, concat_axis=0, tiled=True)
        my_waves = lax.dynamic_slice_in_dim(wave_of_slot, tile_index * per_tile, per_tile)
        flat_matched = matched.reshape(per_tile * 2, nb_dev)
        angle = phases(
            my_waves, jnp.int32(0) // P_SIZE, lax.axis_size("tile") * na_dev // P_SIZE, span, points
        )
        table = jnp.stack([jnp.cos(angle).T, jnp.sin(angle).T], axis=2).reshape(
            lax.axis_size("tile") * na_dev, per_tile * 2
        )
        total = lax.psum_scatter(
            jnp.dot(table, flat_matched, precision=highest), "tile", scatter_dimension=0, tiled=True
        )
        return -total

    def tendency(parts):
        rhs = []
        for component in range(3):
            slopes = [derive(parts[component], direction, False) for direction in range(3)]
            stretch = (
                parts[0] * grad_flow[component][0]
                + parts[1] * grad_flow[component][1]
                + parts[2] * grad_flow[component][2]
            )
            carried = (
                flow_parts[0] * slopes[0] + flow_parts[1] * slopes[1] + flow_parts[2] * slopes[2]
            )
            spread = (
                derive(mass3 * slopes[0], 0, True)
                + derive(mass3 * slopes[1], 1, True)
                + derive(mass3 * slopes[2], 2, True)
            )
            rhs.append(mass3 * (stretch - carried) - diffusivity * spread)
        flux = surface_flux(parts[0][radial_nodes - 1])
        rhs[0] = rhs[0].at[radial_nodes - 1].add(diffusivity * surface_weight * flux)
        stacked = jnp.stack(rhs)
        plane_r = jnp.zeros_like(lax.slice_in_dim(stacked, 0, 1, axis=1))
        stacked = assemble_dim(stacked, 1, plane_r, plane_r)
        padded = padded_2(stacked.astype(jnp.bfloat16), (("tile", 2), ("deg", 3)), 1).astype(
            stacked.dtype
        )
        padded = padded * column_mask
        along_a = assemble_dim(padded[:, :, 1:-1, :], 2, padded[:, :, 0:1, :], padded[:, :, -1:, :])
        along_b = assemble_dim(
            along_a[:, :, :, 1:-1], 3, along_a[:, :, :, 0:1], along_a[:, :, :, -1:]
        )
        return along_b / assembled[None]

    section = field + time_step * tendency([field[0], field[1], field[2]])
    return 0.5 * (field + section + time_step * tendency([section[0], section[1], section[2]]))


def solution(mesh):
    placed = (
        P(None, None, "tile", "deg"),
        P(None, None, "tile", "deg"),
        P(("tile", "deg"), None, None),
        P(),
    )
    return jax.shard_map(
        local, mesh=mesh, in_specs=placed, out_specs=P(None, None, "tile", "deg"), check_vma=False
    )
```

profile of v0, /device:TPU:0, one launch (start us, length us, event | category | flops | bytes accessed | tf_op | source)
XLA Modules:
  0.0 227.2 jit_solution(8538211180107501560)
XLA Ops:
  11.2 30.3 %all-reduce = bf16[32,2,128]{2,0,1:T(8,128)(2,1)S(1)} all-reduce(f32[32,2,128]{2,0,1:T(8,128)S(1)} %fusion.116), channel_id=2, replica_groups=mesh['tile'=8,'deg'=4] {'tile'}, use_global_device_ids=true, to_apply=%region_0.1.clone | all-reduce | flops 8192 | bytes 49152
  41.5 1.2 dynamic-slice.16
  43.9 3.7 %all-to-all-start = ((bf16[4,2,128]{2,1,0:T(2,128)(2,1)}), bf16[4,2,128]{2,1,0:T(2,128)(2,1)S(1)}, u32[]{:S(2)}, u32[]{:S(2)}) async-start(bf16[4,2,128]{2,1,0:T(2,128)(2,1)} %copy.334), calls=%async_computation | async-start | bytes 4096 | tf_op jit(solution)/shard_map/all_to_all | solution.py:164
  64.6 4.2 %all-to-all-start.1 = ((f32[4,1,256]{2,1,0:T(1,128)}), f32[4,1,256]{2,1,0:T(1,128)S(1)}, u32[]{:S(2)}, u32[]{:S(2)}) async-start(f32[4,1,256]{2,1,0:T(1,128)} %reshape.1012), calls=%async_computation.1 | async-start | bytes 8192 | tf_op jit(solution)/shard_map/all_to_all | solution.py:168
  68.8 4.7 %all-to-all-done.1 = f32[4,1,256]{2,1,0:T(1,128)S(1)} async-done(((f32[4,1,256]{2,1,0:T(1,128)}), f32[4,1,256]{2,1,0:T(1,128)S(1)}, u32[]{:S(2)}, u32[]{:S(2)}) %all-to-all-start.1) | async-done | bytes 4128 | tf_op jit(solution)/shard_map/all_to_all | solution.py:168
  76.1 25.9 %reduce-scatter.5.cloned.1.call-done = f32[16,128]{1,0:T(8,128)} async-done(((f32[128,128]{1,0:T(8,128)}), f32[16,128]{1,0:T(8,128)}) %reduce-scatter.5.cloned.1.call-update) | async-done | bytes 8208 | tf_op jit(solution)/shard_map/reduce_scatter | solution.py:177
  104.4 3.5 %collective-permute-done = bf16[3,8,1,128]{3,1,2,0:T(8,128)(2,1)S(1)} collective-permute-done((bf16[3,8,1,128]{3,1,2,0:T(8,128)(2,1)S(1)}, bf16[3,8,1,128]{3,1,2,0:T(8,128)(2,1)S(1)}, u32[]{:S(2)}, u32[]{:S(2)}) %collective-permute-start) | collective-permute-done | bytes 6176 | tf_op jit(solution)/shard_map/ppermute | solution.py:21
  108.0 2.7 %collective-permute-start.3 = (bf16[3,8,18,1]{3,1,2,0:T(8,128)(2,1)S(1)}, bf16[3,8,18,1]{3,1,2,0:T(8,128)(2,1)S(1)}, u32[]{:S(2)}, u32[]{:S(2)}) collective-permute-start(bf16[3,8,18,1]{3,1,2,0:T(8,128)(2,1)S(1)} %get-tuple-element.73), channel_id=1, source_target_pairs={{1,0},{2,1},{3,2},{0,3},{5,4},{6,5},{7,6},{4,7},{9,8},{10,9},{11,1... | collective-permute-start | bytes 2600 | tf_op jit(solution)/shard_map/ppermute | solution.py:22
  110.8 2.2 collective-permute-done.3
  113.0 3.3 %collective-permute-done.2 = bf16[3,8,18,1]{3,1,2,0:T(8,128)(2,1)S(1)} collective-permute-done((bf16[3,8,18,1]{3,1,2,0:T(8,128)(2,1)S(1)}, bf16[3,8,18,1]{3,1,2,0:T(8,128)(2,1)S(1)}, u32[]{:S(2)}, u32[]{:S(2)}) %collective-permute-start.2) | collective-permute-done | bytes 896 | tf_op jit(solution)/shard_map/ppermute | solution.py:21
  117.7 1.3 slice.297
  120.0 2.0 maximum_bitcast_fusion
  126.1 26.0 %all-reduce.1 = bf16[32,2,128]{2,0,1:T(8,128)(2,1)S(1)} all-reduce(f32[32,2,128]{2,0,1:T(8,128)S(1)} %fusion.115), channel_id=4, replica_groups=mesh['tile'=8,'deg'=4] {'tile'}, use_global_device_ids=true, to_apply=%region_2.3.clone | all-reduce | flops 8192 | bytes 49152
  152.7 3.2 %all-to-all-start.2 = ((bf16[4,2,128]{2,1,0:T(2,128)(2,1)}), bf16[4,2,128]{2,1,0:T(2,128)(2,1)S(1)}, u32[]{:S(2)}, u32[]{:S(2)}) async-start(bf16[4,2,128]{2,1,0:T(2,128)(2,1)} %copy.387), calls=%async_computation.3 | async-start | bytes 4096 | tf_op jit(solution)/shard_map/all_to_all | solution.py:164
  156.9 3.5 %all-to-all-done.2 = bf16[4,2,128]{2,1,0:T(2,128)(2,1)S(1)} async-done(((bf16[4,2,128]{2,1,0:T(2,128)(2,1)}), bf16[4,2,128]{2,1,0:T(2,128)(2,1)S(1)}, u32[]{:S(2)}, u32[]{:S(2)}) %all-to-all-start.2) | async-done | bytes 2080 | tf_op jit(solution)/shard_map/all_to_all | solution.py:164
  162.7 3.2 %all-to-all-start.3 = ((f32[4,1,256]{2,1,0:T(1,128)}), f32[4,1,256]{2,1,0:T(1,128)S(1)}, u32[]{:S(2)}, u32[]{:S(2)}) async-start(f32[4,1,256]{2,1,0:T(1,128)} %reshape.1014), calls=%async_computation.4 | async-start | bytes 8192 | tf_op jit(solution)/shard_map/all_to_all | solution.py:168
  166.3 4.3 %all-to-all-done.3 = f32[4,1,256]{2,1,0:T(1,128)S(1)} async-done(((f32[4,1,256]{2,1,0:T(1,128)}), f32[4,1,256]{2,1,0:T(1,128)S(1)}, u32[]{:S(2)}, u32[]{:S(2)}) %all-to-all-start.3) | async-done | bytes 4128 | tf_op jit(solution)/shard_map/all_to_all | solution.py:168
  172.9 26.3 %reduce-scatter.7.cloned.1.call-done = f32[16,128]{1,0:T(8,128)} async-done(((f32[128,128]{1,0:T(8,128)}), f32[16,128]{1,0:T(8,128)}) %reduce-scatter.7.cloned.1.call-update) | async-done | bytes 8208 | tf_op jit(solution)/shard_map/reduce_scatter | solution.py:177
  201.6 3.5 %collective-permute-done.4 = bf16[3,8,1,128]{3,1,2,0:T(8,128)(2,1)S(1)} collective-permute-done((bf16[3,8,1,128]{3,1,2,0:T(8,128)(2,1)S(1)}, bf16[3,8,1,128]{3,1,2,0:T(8,128)(2,1)S(1)}, u32[]{:S(2)}, u32[]{:S(2)}) %collective-permute-start.4) | collective-permute-done | bytes 6176 | tf_op jit(solution)/shard_map/ppermute | solution.py:21
  205.2 2.7 %collective-permute-start.7 = (bf16[3,8,18,1]{3,1,2,0:T(8,128)(2,1)S(1)}, bf16[3,8,18,1]{3,1,2,0:T(8,128)(2,1)S(1)}, u32[]{:S(2)}, u32[]{:S(2)}) collective-permute-start(bf16[3,8,18,1]{3,1,2,0:T(8,128)(2,1)S(1)} %get-tuple-element.71), channel_id=1, source_target_pairs={{1,0},{2,1},{3,2},{0,3},{5,4},{6,5},{7,6},{4,7},{9,8},{10,9},{11,1... | collective-permute-start | bytes 2600 | tf_op jit(solution)/shard_map/ppermute | solution.py:22
  207.9 2.3 %collective-permute-done.7 = bf16[3,8,18,1]{3,1,2,0:T(8,128)(2,1)S(1)} collective-permute-done((bf16[3,8,18,1]{3,1,2,0:T(8,128)(2,1)S(1)}, bf16[3,8,18,1]{3,1,2,0:T(8,128)(2,1)S(1)}, u32[]{:S(2)}, u32[]{:S(2)}) %collective-permute-start.7) | collective-permute-done | bytes 896 | tf_op jit(solution)/shard_map/ppermute | solution.py:22
  210.2 3.3 %collective-permute-done.6 = bf16[3,8,18,1]{3,1,2,0:T(8,128)(2,1)S(1)} collective-permute-done((bf16[3,8,18,1]{3,1,2,0:T(8,128)(2,1)S(1)}, bf16[3,8,18,1]{3,1,2,0:T(8,128)(2,1)S(1)}, u32[]{:S(2)}, u32[]{:S(2)}) %collective-permute-start.6) | collective-permute-done | bytes 896 | tf_op jit(solution)/shard_map/ppermute | solution.py:21
  214.8 1.3 slice.320
  217.1 2.0 maximum_bitcast_fusion.1
  (232 shorter events, 44.9 us)
Async XLA Ops:
  6.5 55.3 %copy-start = (bf16[1,512,512]{2,1,0:T(8,128)(2,1)S(1)}, bf16[1,512,512]{2,1,0:T(8,128)(2,1)}, u32[]{:S(2)}) copy-start(bf16[1,512,512]{2,1,0:T(8,128)(2,1)} %param.13) | copy-start | bytes 1572868
  8.7 39.7 %copy-start.32 = (f32[16]{0:T(128)}, f32[16]{0:T(128)S(1)}, u32[]{:S(2)}) copy-start(f32[16]{0:T(128)S(1)} %get-tuple-element.95) | copy-start | bytes 196
  43.9 17.9 %all-to-all-start = ((bf16[4,2,128]{2,1,0:T(2,128)(2,1)}), bf16[4,2,128]{2,1,0:T(2,128)(2,1)S(1)}, u32[]{:S(2)}, u32[]{:S(2)}) async-start(bf16[4,2,128]{2,1,0:T(2,128)(2,1)} %copy.334), calls=%async_computation | async-start | bytes 4096 | tf_op jit(solution)/shard_map/all_to_all | solution.py:164
  48.5 12.3 %copy-start.24 = (f32[8,2,8]{2,1,0:T(2,128)}, f32[8,2,8]{2,1,0:T(2,128)S(1)}, u32[]{:S(2)}) copy-start(f32[8,2,8]{2,1,0:T(2,128)S(1)} %broadcast_multiply_fusion.3) | copy-start | bytes 1540
  49.4 6.3 %copy-start.2 = (f32[3,8,16,128]{3,2,1,0:T(8,128)S(1)}, f32[3,8,16,128]{3,2,1,0:T(8,128)}, u32[]{:S(2)}) copy-start(f32[3,8,16,128]{3,2,1,0:T(8,128)} %param.12) | copy-start | bytes 589828
  49.4 6.5 %copy-start.1 = (f32[3,8,16,128]{3,2,1,0:T(8,128)S(1)}, f32[3,8,16,128]{3,2,1,0:T(8,128)}, u32[]{:S(2)}) copy-start(f32[3,8,16,128]{3,2,1,0:T(8,128)} %param.11) | copy-start | bytes 589828
  51.6 7.2 %copy-start.10 = (f32[8,16,128]{2,1,0:T(8,128)}, f32[8,16,128]{2,1,0:T(8,128)S(1)}, u32[]{:S(2)}) copy-start(f32[8,16,128]{2,1,0:T(8,128)S(1)} %convolution_bitcast_fusion.6) | copy-start | bytes 196612
  51.6 4.9 %copy-start.22 = (f32[8,8,1,1]{1,0,3,2:T(8,128)S(1)}, f32[8,8,1,1]{1,0,3,2:T(8,128)}, u32[]{:S(2)}) copy-start(f32[8,8,1,1]{1,0,3,2:T(8,128)} %constant.239) | copy-start | bytes 772
  56.5 19.0 %copy-start.6 = (f32[8,16,128]{2,1,0:T(8,128)}, f32[8,16,128]{2,1,0:T(8,128)S(1)}, u32[]{:S(2)}) copy-start(f32[8,16,128]{2,1,0:T(8,128)S(1)} %convolution_bitcast_fusion.9) | copy-start | bytes 196612
  59.5 16.0 %copy-start.16 = (f32[8,16,128]{2,0,1:T(8,128)}, f32[8,16,128]{2,0,1:T(8,128)S(1)}, u32[]{:S(2)}) copy-start(f32[8,16,128]{2,0,1:T(8,128)S(1)} %fusion.84) | copy-start | bytes 196612
  61.8 14.1 %copy-start.20 = (f32[8,16,128]{2,1,0:T(8,128)}, f32[8,16,128]{2,1,0:T(8,128)S(1)}, u32[]{:S(2)}) copy-start(f32[8,16,128]{2,1,0:T(8,128)S(1)} %convolution_bitcast_fusion.10) | copy-start | bytes 196612
  64.6 8.9 %all-to-all-start.1 = ((f32[4,1,256]{2,1,0:T(1,128)}), f32[4,1,256]{2,1,0:T(1,128)S(1)}, u32[]{:S(2)}, u32[]{:S(2)}) async-start(f32[4,1,256]{2,1,0:T(1,128)} %reshape.1012), calls=%async_computation.1 | async-start | bytes 8192 | tf_op jit(solution)/shard_map/all_to_all | solution.py:168
  68.8 33.2 %reduce-scatter.5.cloned.1.call-start = ((), (), s32[]{:S(2)}) async-start(), calls=%async_computation.6 | async-start | bytes 73728 | tf_op jit(solution)/shard_map/reduce_scatter | solution.py:177
  102.8 1.5 collective-permute-start.1
  103.0 4.9 %collective-permute-start = (bf16[3,8,1,128]{3,1,2,0:T(8,128)(2,1)S(1)}, bf16[3,8,1,128]{3,1,2,0:T(8,128)(2,1)S(1)}, u32[]{:S(2)}, u32[]{:S(2)}) collective-permute-start(bf16[3,8,1,128]{3,1,2,0:T(8,128)(2,1)S(1)} %get-tuple-element.76), channel_id=1, source_target_pairs={{0,4},{4,8},{8,12},{12,16},{16,20},{20,24},{24,28},{28,0},{1,5},{5... | collective-permute-start | bytes 18440 | tf_op jit(solution)/shard_map/ppermute | solution.py:21
  108.0 5.0 %collective-permute-start.3 = (bf16[3,8,18,1]{3,1,2,0:T(8,128)(2,1)S(1)}, bf16[3,8,18,1]{3,1,2,0:T(8,128)(2,1)S(1)}, u32[]{:S(2)}, u32[]{:S(2)}) collective-permute-start(bf16[3,8,18,1]{3,1,2,0:T(8,128)(2,1)S(1)} %get-tuple-element.73), channel_id=1, source_target_pairs={{1,0},{2,1},{3,2},{0,3},{5,4},{6,5},{7,6},{4,7},{9,8},{10,9},{11,1... | collective-permute-start | bytes 2600 | tf_op jit(solution)/shard_map/ppermute | solution.py:22
  110.7 5.6 %collective-permute-start.2 = (bf16[3,8,18,1]{3,1,2,0:T(8,128)(2,1)S(1)}, bf16[3,8,18,1]{3,1,2,0:T(8,128)(2,1)S(1)}, u32[]{:S(2)}, u32[]{:S(2)}) collective-permute-start(bf16[3,8,18,1]{3,1,2,0:T(8,128)(2,1)S(1)} %get-tuple-element.72), channel_id=1, source_target_pairs={{0,1},{1,2},{2,3},{3,0},{4,5},{5,6},{6,7},{7,4},{8,9},{9,10},{10,1... | collective-permute-start | bytes 2600 | tf_op jit(solution)/shard_map/ppermute | solution.py:21
  152.7 7.8 %all-to-all-start.2 = ((bf16[4,2,128]{2,1,0:T(2,128)(2,1)}), bf16[4,2,128]{2,1,0:T(2,128)(2,1)S(1)}, u32[]{:S(2)}, u32[]{:S(2)}) async-start(bf16[4,2,128]{2,1,0:T(2,128)(2,1)} %copy.387), calls=%async_computation.3 | async-start | bytes 4096 | tf_op jit(solution)/shard_map/all_to_all | solution.py:164
  162.7 7.9 %all-to-all-start.3 = ((f32[4,1,256]{2,1,0:T(1,128)}), f32[4,1,256]{2,1,0:T(1,128)S(1)}, u32[]{:S(2)}, u32[]{:S(2)}) async-start(f32[4,1,256]{2,1,0:T(1,128)} %reshape.1014), calls=%async_computation.4 | async-start | bytes 8192 | tf_op jit(solution)/shard_map/all_to_all | solution.py:168
  166.0 33.2 %reduce-scatter.7.cloned.1.call-start = ((), (), s32[]{:S(2)}) async-start(), calls=%async_computation.7 | async-start | bytes 73728 | tf_op jit(solution)/shard_map/reduce_scatter | solution.py:177
  200.0 1.5 collective-permute-start.5
  200.2 4.9 %collective-permute-start.4 = (bf16[3,8,1,128]{3,1,2,0:T(8,128)(2,1)S(1)}, bf16[3,8,1,128]{3,1,2,0:T(8,128)(2,1)S(1)}, u32[]{:S(2)}, u32[]{:S(2)}) collective-permute-start(bf16[3,8,1,128]{3,1,2,0:T(8,128)(2,1)S(1)} %get-tuple-element.74), channel_id=1, source_target_pairs={{0,4},{4,8},{8,12},{12,16},{16,20},{20,24},{24,28},{28,0},{1,5},{5... | collective-permute-start | bytes 18440 | tf_op jit(solution)/shard_map/ppermute | solution.py:21
  205.2 5.0 %collective-permute-start.7 = (bf16[3,8,18,1]{3,1,2,0:T(8,128)(2,1)S(1)}, bf16[3,8,18,1]{3,1,2,0:T(8,128)(2,1)S(1)}, u32[]{:S(2)}, u32[]{:S(2)}) collective-permute-start(bf16[3,8,18,1]{3,1,2,0:T(8,128)(2,1)S(1)} %get-tuple-element.71), channel_id=1, source_target_pairs={{1,0},{2,1},{3,2},{0,3},{5,4},{6,5},{7,6},{4,7},{9,8},{10,9},{11,1... | collective-permute-start | bytes 2600 | tf_op jit(solution)/shard_map/ppermute | solution.py:22
  207.9 5.6 %collective-permute-start.6 = (bf16[3,8,18,1]{3,1,2,0:T(8,128)(2,1)S(1)}, bf16[3,8,18,1]{3,1,2,0:T(8,128)(2,1)S(1)}, u32[]{:S(2)}, u32[]{:S(2)}) collective-permute-start(bf16[3,8,18,1]{3,1,2,0:T(8,128)(2,1)S(1)} %get-tuple-element.70), channel_id=1, source_target_pairs={{0,1},{1,2},{2,3},{3,0},{4,5},{5,6},{6,7},{7,4},{8,9},{9,10},{10,1... | collective-permute-start | bytes 2600 | tf_op jit(solution)/shard_map/ppermute | solution.py:21
  (24 other events, 50.7 us)
Sparse Core Ops, SparseCore 0:
  75.7 26.3 reduce-scatter.4
  172.8 26.3 reduce-scatter.6
where the time goes:
time: 228 us; the launch traced here: 227 us
  waiting for transfers between devices  84.8 us (37%)
  blocking collectives  56.3 us (25%)
  starting transfers between devices  21 us (9%)
  local copies, waits for them, and re-layouts  17.1 us (8%)
  matrix products  16.9 us (7%)
  other arithmetic  15.9 us (7%)
  between operations  15.3 us (7%)
    unnamed x2, blocking collectives  56.3 us
    reduce_scatter x2, waiting for transfers between devices, surface_flux(): lax.psum_scatter(jnp.dot(table, flat_matched, precision=highest), 'tile',...  52.2 us
    ppermute x4, waiting for transfers between devices, padded_2(): before = lax.ppermute(last, axis, up)  13.6 us
    dot_general x30, matrix products, apply_along(): return jnp.einsum(formula, blocks, matrix, precision=highest).reshape(shape)  9.26 us
    all_to_all x2, waiting for transfers between devices, surface_flux(): lax.all_to_all(mapped, 'deg', split_axis=2, concat_axis=0, tiled=True)  8.98 us
    all_to_all x2, starting transfers between devices, surface_flux(): lax.all_to_all(mapped, 'deg', split_axis=2, concat_axis=0, tiled=True)  7.44 us
    all_to_all x2, starting transfers between devices, surface_flux(): lax.all_to_all(coeff.astype(jnp.bfloat16), 'deg', split_axis=0, concat_ax...  6.94 us
    unnamed x81, local copies, waits for them, and re-layouts  6.64 us
  transfers between devices with their start and end apart: 14, of which 13 were waited for; matrix products, arithmetic and copies ran while one was open for 7% of the time, Pallas kernels for 0%

commit v1 on v0

--- a/solution.py
+++ b/solution.py
@@ -9,6 +9,18 @@
 time_step = 0.01
 highest = lax.Precision.HIGHEST
 gll_interior = [0.2092992179024789, 0.5917001814331423, 0.8717401485096066]
+
+
+def cut_along(value, dim, size):
+    shape = value.shape
+    blocks = value.reshape(*shape[:dim], size, shape[dim] // size, *shape[dim + 1 :])
+    return jnp.moveaxis(blocks, dim, 0)
+
+
+def joined_along(pieces, dim):
+    pieces = jnp.moveaxis(pieces, 0, dim)
+    shape = pieces.shape
+    return pieces.reshape(*shape[:dim], shape[dim] * shape[dim + 1], *shape[dim + 2 :])
 
 
 def padded_2(value, sides, width):
@@ -165,7 +177,18 @@
             coeff.astype(jnp.bfloat16), "deg", split_axis=0, concat_axis=2, tiled=True
         )
         mapped = jnp.einsum("kpq,kcq->kcp", match_ops, owned, preferred_element_type=jnp.float32)
-        matched = lax.all_to_all(mapped, "deg", split_axis=2, concat_axis=0, tiled=True)
+        length_2, here = (lax.axis_size("deg"), lax.axis_index("deg"))
+        tiles_2 = cut_along(mapped, 2, length_2)
+        outs = [tiles_2[here]]
+        for step in range(1, length_2):
+            sent = tiles_2[(here + step) % length_2]
+            outs.append(
+                lax.ppermute(
+                    sent, "deg", [(i_2, (i_2 + step) % length_2) for i_2 in range(length_2)]
+                )
+            )
+        tiles_2 = jnp.stack(outs)[(here - jnp.arange(length_2)) % length_2]
+        matched = joined_along(tiles_2, 0)
         my_waves = lax.dynamic_slice_in_dim(wave_of_slot, tile_index * per_tile, per_tile)
         flat_matched = matched.reshape(per_tile * 2, nb_dev)
         angle = phases(

time: 228 us -> 221 us (0.969)
  other arithmetic: 15.9 us -> 12.3 us
    all_to_all x2 -> x0, waiting for transfers between devices: 8.98 us -> none  [surface_flux(): lax.all_to_all(mapped, 'deg', split_axis=2, concat_axis=0, tiled=True)]
    ppermute x0 -> x6, waiting for transfers between devices: none -> 7.52 us  [surface_flux(): lax.ppermute(sent, 'deg', [(i_2, (i_2 + step) % length_2) for i_2 in rang...]
    all_to_all x2 -> x0, starting transfers between devices: 7.44 us -> none  [surface_flux(): lax.all_to_all(mapped, 'deg', split_axis=2, concat_axis=0, tiled=True)]
    ppermute x0 -> x6, starting transfers between devices: none -> 6.83 us  [surface_flux(): lax.ppermute(sent, 'deg', [(i_2, (i_2 + step) % length_2) for i_2 in rang...]
    unnamed x81 -> x80, local copies, waits for them, and re-layouts: 6.64 us -> 3.8 us
    unnamed x2 -> x0, other arithmetic: 2.44 us -> none
  transfers between devices with their start and end apart: 14 -> 18, of which waited for: 13 -> 17; matrix products, arithmetic and copies ran while one was open for 7% -> 7% of each run, Pallas kernels for 0% -> 0%
where the time goes in v1:
time: 221 us; the launch traced here: 220 us
  waiting for transfers between devices  84.1 us (38%)
  blocking collectives  56.3 us (25%)
  starting transfers between devices  20.3 us (9%)
  matrix products  16.8 us (8%)
  between operations  15.3 us (7%)
  local copies, waits for them, and re-layouts  15.2 us (7%)
  other arithmetic  12.3 us (6%)
    unnamed x2, blocking collectives  56.3 us
    reduce_scatter x2, waiting for transfers between devices, surface_flux(): lax.psum_scatter(jnp.dot(table, flat_matched, precision=highest), 'tile',...  53.1 us
    ppermute x4, waiting for transfers between devices, padded_2(): before = lax.ppermute(last, axis, up)  13.6 us
    dot_general x30, matrix products, apply_along(): return jnp.einsum(formula, blocks, matrix, precision=highest).reshape(shape)  9.27 us
    ppermute x6, waiting for transfers between devices, surface_flux(): lax.ppermute(sent, 'deg', [(i_2, (i_2 + step) % length_2) for i_2 in rang...  7.52 us
    all_to_all x2, starting transfers between devices, surface_flux(): lax.all_to_all(coeff.astype(jnp.bfloat16), 'deg', split_axis=0, concat_ax...  6.94 us
    ppermute x6, starting transfers between devices, surface_flux(): lax.ppermute(sent, 'deg', [(i_2, (i_2 + step) % length_2) for i_2 in rang...  6.83 us
    ppermute x4, waiting for transfers between devices, padded_2(): after = lax.ppermute(first, axis, down)  6.39 us
  transfers between devices with their start and end apart: 18, of which 17 were waited for; matrix products, arithmetic and copies ran while one was open for 7% of the time, Pallas kernels for 0%

profile of v1, /device:TPU:0, one launch (start us, length us, event | category | flops | bytes accessed | tf_op | source)
XLA Modules:
  0.0 220.3 jit_solution(5791490967847780379)
XLA Ops:
  11.2 30.3 %all-reduce = bf16[32,2,128]{2,0,1:T(8,128)(2,1)S(1)} all-reduce(f32[32,2,128]{2,0,1:T(8,128)S(1)} %fusion.112), channel_id=2, replica_groups=mesh['tile'=8,'deg'=4] {'tile'}, use_global_device_ids=true, to_apply=%region_0.1.clone | all-reduce | flops 8192 | bytes 49152
  43.9 3.7 %all-to-all-start = ((bf16[4,2,128]{2,1,0:T(2,128)(2,1)}), bf16[4,2,128]{2,1,0:T(2,128)(2,1)S(1)}, u32[]{:S(2)}, u32[]{:S(2)}) async-start(bf16[4,2,128]{2,1,0:T(2,128)(2,1)} %copy.328), calls=%async_computation | async-start | bytes 4096 | tf_op jit(solution)/shard_map/all_to_all | solution.py:176
  62.1 2.9 %collective-permute-start.2 = (f32[1,2,128]{2,1,0:T(2,128)S(1)}, f32[1,2,128]{2,1,0:T(2,128)S(1)}, u32[]{:S(2)}, u32[]{:S(2)}) collective-permute-start(f32[1,2,128]{2,1,0:T(2,128)S(1)} %get-tuple-element.95), channel_id=1, source_target_pairs={{0,3},{1,0},{2,1},{3,2},{4,7},{5,4},{6,5},{7,6},{8,11},{9,8},{10,9... | collective-permute-start | bytes 3080 | tf_op jit(solution)/shard_map/ppermute | solution.py:186
  66.4 2.3 %collective-permute-done.1 = f32[1,2,128]{2,1,0:T(2,128)S(1)} collective-permute-done((f32[1,2,128]{2,1,0:T(2,128)S(1)}, f32[1,2,128]{2,1,0:T(2,128)S(1)}, u32[]{:S(2)}, u32[]{:S(2)}) %collective-permute-start.1) | collective-permute-done | bytes 1056 | tf_op jit(solution)/shard_map/ppermute | solution.py:186
  68.6 1.5 collective-permute-done
  72.2 26.8 %reduce-scatter.5.cloned.1.call-done = f32[16,128]{1,0:T(8,128)} async-done(((f32[128,128]{1,0:T(8,128)}), f32[16,128]{1,0:T(8,128)}) %reduce-scatter.5.cloned.1.call-update) | async-done | bytes 8208 | tf_op jit(solution)/shard_map/reduce_scatter | solution.py:200
  101.3 3.5 %collective-permute-done.3 = bf16[3,8,1,128]{3,1,2,0:T(8,128)(2,1)S(1)} collective-permute-done((bf16[3,8,1,128]{3,1,2,0:T(8,128)(2,1)S(1)}, bf16[3,8,1,128]{3,1,2,0:T(8,128)(2,1)S(1)}, u32[]{:S(2)}, u32[]{:S(2)}) %collective-permute-start.3) | collective-permute-done | bytes 6176 | tf_op jit(solution)/shard_map/ppermute | solution.py:33
  105.0 2.7 %collective-permute-start.6 = (bf16[3,8,18,1]{3,1,2,0:T(8,128)(2,1)S(1)}, bf16[3,8,18,1]{3,1,2,0:T(8,128)(2,1)S(1)}, u32[]{:S(2)}, u32[]{:S(2)}) collective-permute-start(bf16[3,8,18,1]{3,1,2,0:T(8,128)(2,1)S(1)} %get-tuple-element.73), channel_id=1, source_target_pairs={{1,0},{2,1},{3,2},{0,3},{5,4},{6,5},{7,6},{4,7},{9,8},{10,9},{11,1... | collective-permute-start | bytes 2600 | tf_op jit(solution)/shard_map/ppermute | solution.py:34
  107.8 2.2 %collective-permute-done.6 = bf16[3,8,18,1]{3,1,2,0:T(8,128)(2,1)S(1)} collective-permute-done((bf16[3,8,18,1]{3,1,2,0:T(8,128)(2,1)S(1)}, bf16[3,8,18,1]{3,1,2,0:T(8,128)(2,1)S(1)}, u32[]{:S(2)}, u32[]{:S(2)}) %collective-permute-start.6) | collective-permute-done | bytes 896 | tf_op jit(solution)/shard_map/ppermute | solution.py:34
  110.0 3.3 %collective-permute-done.5 = bf16[3,8,18,1]{3,1,2,0:T(8,128)(2,1)S(1)} collective-permute-done((bf16[3,8,18,1]{3,1,2,0:T(8,128)(2,1)S(1)}, bf16[3,8,18,1]{3,1,2,0:T(8,128)(2,1)S(1)}, u32[]{:S(2)}, u32[]{:S(2)}) %collective-permute-start.5) | collective-permute-done | bytes 896 | tf_op jit(solution)/shard_map/ppermute | solution.py:33
  114.6 1.3 slice.301
  116.9 2.0 maximum_bitcast_fusion
  123.1 26.0 %all-reduce.1 = bf16[32,2,128]{2,0,1:T(8,128)(2,1)S(1)} all-reduce(f32[32,2,128]{2,0,1:T(8,128)S(1)} %fusion.111), channel_id=4, replica_groups=mesh['tile'=8,'deg'=4] {'tile'}, use_global_device_ids=true, to_apply=%region_2.3.clone | all-reduce | flops 8192 | bytes 49152
  149.6 3.2 %all-to-all-start.1 = ((bf16[4,2,128]{2,1,0:T(2,128)(2,1)}), bf16[4,2,128]{2,1,0:T(2,128)(2,1)S(1)}, u32[]{:S(2)}, u32[]{:S(2)}) async-start(bf16[4,2,128]{2,1,0:T(2,128)(2,1)} %copy.379), calls=%async_computation.2 | async-start | bytes 4096 | tf_op jit(solution)/shard_map/all_to_all | solution.py:176
  153.9 3.4 %all-to-all-done.1 = bf16[4,2,128]{2,1,0:T(2,128)(2,1)S(1)} async-done(((bf16[4,2,128]{2,1,0:T(2,128)(2,1)}), bf16[4,2,128]{2,1,0:T(2,128)(2,1)S(1)}, u32[]{:S(2)}, u32[]{:S(2)}) %all-to-all-start.1) | async-done | bytes 2080 | tf_op jit(solution)/shard_map/all_to_all | solution.py:176
  158.3 1.5 collective-permute-start.8
  161.9 2.4 %collective-permute-done.7 = f32[1,2,128]{2,1,0:T(2,128)S(1)} collective-permute-done((f32[1,2,128]{2,1,0:T(2,128)S(1)}, f32[1,2,128]{2,1,0:T(2,128)S(1)}, u32[]{:S(2)}, u32[]{:S(2)}) %collective-permute-start.7) | collective-permute-done | bytes 1056 | tf_op jit(solution)/shard_map/ppermute | solution.py:186
  166.0 26.3 %reduce-scatter.7.cloned.1.call-done = f32[16,128]{1,0:T(8,128)} async-done(((f32[128,128]{1,0:T(8,128)}), f32[16,128]{1,0:T(8,128)}) %reduce-scatter.7.cloned.1.call-update) | async-done | bytes 8208 | tf_op jit(solution)/shard_map/reduce_scatter | solution.py:200
  194.7 3.5 %collective-permute-done.10 = bf16[3,8,1,128]{3,1,2,0:T(8,128)(2,1)S(1)} collective-permute-done((bf16[3,8,1,128]{3,1,2,0:T(8,128)(2,1)S(1)}, bf16[3,8,1,128]{3,1,2,0:T(8,128)(2,1)S(1)}, u32[]{:S(2)}, u32[]{:S(2)}) %collective-permute-start.10) | collective-permute-done | bytes 6176 | tf_op jit(solution)/shard_map/ppermute | solution.py:33
  198.3 2.7 %collective-permute-start.13 = (bf16[3,8,18,1]{3,1,2,0:T(8,128)(2,1)S(1)}, bf16[3,8,18,1]{3,1,2,0:T(8,128)(2,1)S(1)}, u32[]{:S(2)}, u32[]{:S(2)}) collective-permute-start(bf16[3,8,18,1]{3,1,2,0:T(8,128)(2,1)S(1)} %get-tuple-element.71), channel_id=1, source_target_pairs={{1,0},{2,1},{3,2},{0,3},{5,4},{6,5},{7,6},{4,7},{9,8},{10,9},{11,1... | collective-permute-start | bytes 2600 | tf_op jit(solution)/shard_map/ppermute | solution.py:34
  201.0 2.3 %collective-permute-done.13 = bf16[3,8,18,1]{3,1,2,0:T(8,128)(2,1)S(1)} collective-permute-done((bf16[3,8,18,1]{3,1,2,0:T(8,128)(2,1)S(1)}, bf16[3,8,18,1]{3,1,2,0:T(8,128)(2,1)S(1)}, u32[]{:S(2)}, u32[]{:S(2)}) %collective-permute-start.13) | collective-permute-done | bytes 896 | tf_op jit(solution)/shard_map/ppermute | solution.py:34
  203.3 3.3 %collective-permute-done.12 = bf16[3,8,18,1]{3,1,2,0:T(8,128)(2,1)S(1)} collective-permute-done((bf16[3,8,18,1]{3,1,2,0:T(8,128)(2,1)S(1)}, bf16[3,8,18,1]{3,1,2,0:T(8,128)(2,1)S(1)}, u32[]{:S(2)}, u32[]{:S(2)}) %collective-permute-start.12) | collective-permute-done | bytes 896 | tf_op jit(solution)/shard_map/ppermute | solution.py:33
  208.0 1.3 slice.324
  210.3 2.0 maximum_bitcast_fusion.1
  (241 shorter events, 44.4 us)
Async XLA Ops:
  6.5 55.3 %copy-start = (bf16[1,512,512]{2,1,0:T(8,128)(2,1)S(1)}, bf16[1,512,512]{2,1,0:T(8,128)(2,1)}, u32[]{:S(2)}) copy-start(bf16[1,512,512]{2,1,0:T(8,128)(2,1)} %param.13) | copy-start | bytes 1572868
  7.3 91.7 %copy-start.30 = (f32[16]{0:T(128)}, f32[16]{0:T(128)S(1)}, u32[]{:S(2)}) copy-start(f32[16]{0:T(128)S(1)} %mul.669) | copy-start | bytes 196
  8.8 39.7 %copy-start.34 = (f32[16]{0:T(128)}, f32[16]{0:T(128)S(1)}, u32[]{:S(2)}) copy-start(f32[16]{0:T(128)S(1)} %get-tuple-element.103) | copy-start | bytes 196
  43.9 17.9 %all-to-all-start = ((bf16[4,2,128]{2,1,0:T(2,128)(2,1)}), bf16[4,2,128]{2,1,0:T(2,128)(2,1)S(1)}, u32[]{:S(2)}, u32[]{:S(2)}) async-start(bf16[4,2,128]{2,1,0:T(2,128)(2,1)} %copy.328), calls=%async_computation | async-start | bytes 4096 | tf_op jit(solution)/shard_map/all_to_all | solution.py:176
  47.7 51.4 %reduce-scatter.5.cloned.1.call-start = ((), (), s32[]{:S(2)}) async-start(), calls=%async_computation.4 | async-start | bytes 73728 | tf_op jit(solution)/shard_map/reduce_scatter | solution.py:200
  56.5 15.1 %copy-start.6 = (f32[8,16,128]{2,1,0:T(8,128)}, f32[8,16,128]{2,1,0:T(8,128)S(1)}, u32[]{:S(2)}) copy-start(f32[8,16,128]{2,1,0:T(8,128)S(1)} %convolution_bitcast_fusion.9) | copy-start | bytes 196612
  56.7 14.9 %copy-start.12 = (f32[8,16,128]{2,1,0:T(8,128)}, f32[8,16,128]{2,1,0:T(8,128)S(1)}, u32[]{:S(2)}) copy-start(f32[8,16,128]{2,1,0:T(8,128)S(1)} %convolution_bitcast_fusion.10) | copy-start | bytes 196612
  62.1 4.2 %collective-permute-start.2 = (f32[1,2,128]{2,1,0:T(2,128)S(1)}, f32[1,2,128]{2,1,0:T(2,128)S(1)}, u32[]{:S(2)}, u32[]{:S(2)}) collective-permute-start(f32[1,2,128]{2,1,0:T(2,128)S(1)} %get-tuple-element.95), channel_id=1, source_target_pairs={{0,3},{1,0},{2,1},{3,2},{4,7},{5,4},{6,5},{7,6},{8,11},{9,8},{10,9... | collective-permute-start | bytes 3080 | tf_op jit(solution)/shard_map/ppermute | solution.py:186
  65.1 3.6 %collective-permute-start.1 = (f32[1,2,128]{2,1,0:T(2,128)S(1)}, f32[1,2,128]{2,1,0:T(2,128)S(1)}, u32[]{:S(2)}, u32[]{:S(2)}) collective-permute-start(f32[1,2,128]{2,1,0:T(2,128)S(1)} %get-tuple-element.96), channel_id=1, source_target_pairs={{0,2},{1,3},{2,0},{3,1},{4,6},{5,7},{6,4},{7,5},{8,10},{9,11},{10,... | collective-permute-start | bytes 3080 | tf_op jit(solution)/shard_map/ppermute | solution.py:186
  65.6 4.5 %collective-permute-start = (f32[1,2,128]{2,1,0:T(2,128)S(1)}, f32[1,2,128]{2,1,0:T(2,128)S(1)}, u32[]{:S(2)}, u32[]{:S(2)}) collective-permute-start(f32[1,2,128]{2,1,0:T(2,128)S(1)} %get-tuple-element.97), channel_id=1, source_target_pairs={{0,1},{1,2},{2,3},{3,0},{4,5},{5,6},{6,7},{7,4},{8,9},{9,10},{10,1... | collective-permute-start | bytes 3080 | tf_op jit(solution)/shard_map/ppermute | solution.py:186
  99.8 1.5 collective-permute-start.4
  100.0 4.9 %collective-permute-start.3 = (bf16[3,8,1,128]{3,1,2,0:T(8,128)(2,1)S(1)}, bf16[3,8,1,128]{3,1,2,0:T(8,128)(2,1)S(1)}, u32[]{:S(2)}, u32[]{:S(2)}) collective-permute-start(bf16[3,8,1,128]{3,1,2,0:T(8,128)(2,1)S(1)} %get-tuple-element.76), channel_id=1, source_target_pairs={{0,4},{4,8},{8,12},{12,16},{16,20},{20,24},{24,28},{28,0},{1,5},{5... | collective-permute-start | bytes 18440 | tf_op jit(solution)/shard_map/ppermute | solution.py:33
  105.0 5.0 %collective-permute-start.6 = (bf16[3,8,18,1]{3,1,2,0:T(8,128)(2,1)S(1)}, bf16[3,8,18,1]{3,1,2,0:T(8,128)(2,1)S(1)}, u32[]{:S(2)}, u32[]{:S(2)}) collective-permute-start(bf16[3,8,18,1]{3,1,2,0:T(8,128)(2,1)S(1)} %get-tuple-element.73), channel_id=1, source_target_pairs={{1,0},{2,1},{3,2},{0,3},{5,4},{6,5},{7,6},{4,7},{9,8},{10,9},{11,1... | collective-permute-start | bytes 2600 | tf_op jit(solution)/shard_map/ppermute | solution.py:34
  107.7 5.6 %collective-permute-start.5 = (bf16[3,8,18,1]{3,1,2,0:T(8,128)(2,1)S(1)}, bf16[3,8,18,1]{3,1,2,0:T(8,128)(2,1)S(1)}, u32[]{:S(2)}, u32[]{:S(2)}) collective-permute-start(bf16[3,8,18,1]{3,1,2,0:T(8,128)(2,1)S(1)} %get-tuple-element.72), channel_id=1, source_target_pairs={{0,1},{1,2},{2,3},{3,0},{4,5},{5,6},{6,7},{7,4},{8,9},{9,10},{10,1... | collective-permute-start | bytes 2600 | tf_op jit(solution)/shard_map/ppermute | solution.py:33
  149.6 7.8 %all-to-all-start.1 = ((bf16[4,2,128]{2,1,0:T(2,128)(2,1)}), bf16[4,2,128]{2,1,0:T(2,128)(2,1)S(1)}, u32[]{:S(2)}, u32[]{:S(2)}) async-start(bf16[4,2,128]{2,1,0:T(2,128)(2,1)} %copy.379), calls=%async_computation.2 | async-start | bytes 4096 | tf_op jit(solution)/shard_map/all_to_all | solution.py:176
  152.9 39.5 %reduce-scatter.7.cloned.1.call-start = ((), (), s32[]{:S(2)}) async-start(), calls=%async_computation.5 | async-start | bytes 73728 | tf_op jit(solution)/shard_map/reduce_scatter | solution.py:200
  152.9 39.4 %copy-start.31 = (f32[16]{0:T(128)S(1)}, f32[16]{0:T(128)}, u32[]{:S(2)}) copy-start(f32[16]{0:T(128)} %copy-done.30) | copy-start | bytes 196
  157.6 3.7 %collective-permute-start.9 = (f32[1,2,128]{2,1,0:T(2,128)S(1)}, f32[1,2,128]{2,1,0:T(2,128)S(1)}, u32[]{:S(2)}, u32[]{:S(2)}) collective-permute-start(f32[1,2,128]{2,1,0:T(2,128)S(1)} %get-tuple-element.91), channel_id=1, source_target_pairs={{0,3},{1,0},{2,1},{3,2},{4,7},{5,4},{6,5},{7,6},{8,11},{9,8},{10,9... | collective-permute-start | bytes 3080 | tf_op jit(solution)/shard_map/ppermute | solution.py:186
  158.3 3.6 %collective-permute-start.8 = (f32[1,2,128]{2,1,0:T(2,128)S(1)}, f32[1,2,128]{2,1,0:T(2,128)S(1)}, u32[]{:S(2)}, u32[]{:S(2)}) collective-permute-start(f32[1,2,128]{2,1,0:T(2,128)S(1)} %get-tuple-element.92), channel_id=1, source_target_pairs={{0,2},{1,3},{2,0},{3,1},{4,6},{5,7},{6,4},{7,5},{8,10},{9,11},{10,... | collective-permute-start | bytes 3080 | tf_op jit(solution)/shard_map/ppermute | solution.py:186
  159.8 4.5 %collective-permute-start.7 = (f32[1,2,128]{2,1,0:T(2,128)S(1)}, f32[1,2,128]{2,1,0:T(2,128)S(1)}, u32[]{:S(2)}, u32[]{:S(2)}) collective-permute-start(f32[1,2,128]{2,1,0:T(2,128)S(1)} %get-tuple-element.93), channel_id=1, source_target_pairs={{0,1},{1,2},{2,3},{3,0},{4,5},{5,6},{6,7},{7,4},{8,9},{9,10},{10,1... | collective-permute-start | bytes 3080 | tf_op jit(solution)/shard_map/ppermute | solution.py:186
  193.2 1.5 collective-permute-start.11
  193.4 4.9 %collective-permute-start.10 = (bf16[3,8,1,128]{3,1,2,0:T(8,128)(2,1)S(1)}, bf16[3,8,1,128]{3,1,2,0:T(8,128)(2,1)S(1)}, u32[]{:S(2)}, u32[]{:S(2)}) collective-permute-start(bf16[3,8,1,128]{3,1,2,0:T(8,128)(2,1)S(1)} %get-tuple-element.74), channel_id=1, source_target_pairs={{0,4},{4,8},{8,12},{12,16},{16,20},{20,24},{24,28},{28,0},{1,5},{5... | collective-permute-start | bytes 18440 | tf_op jit(solution)/shard_map/ppermute | solution.py:33
  198.3 5.0 %collective-permute-start.13 = (bf16[3,8,18,1]{3,1,2,0:T(8,128)(2,1)S(1)}, bf16[3,8,18,1]{3,1,2,0:T(8,128)(2,1)S(1)}, u32[]{:S(2)}, u32[]{:S(2)}) collective-permute-start(bf16[3,8,18,1]{3,1,2,0:T(8,128)(2,1)S(1)} %get-tuple-element.71), channel_id=1, source_target_pairs={{1,0},{2,1},{3,2},{0,3},{5,4},{6,5},{7,6},{4,7},{9,8},{10,9},{11,1... | collective-permute-start | bytes 2600 | tf_op jit(solution)/shard_map/ppermute | solution.py:34
  201.0 5.6 %collective-permute-start.12 = (bf16[3,8,18,1]{3,1,2,0:T(8,128)(2,1)S(1)}, bf16[3,8,18,1]{3,1,2,0:T(8,128)(2,1)S(1)}, u32[]{:S(2)}, u32[]{:S(2)}) collective-permute-start(bf16[3,8,18,1]{3,1,2,0:T(8,128)(2,1)S(1)} %get-tuple-element.70), channel_id=1, source_target_pairs={{0,1},{1,2},{2,3},{3,0},{4,5},{5,6},{6,7},{7,4},{8,9},{9,10},{10,1... | collective-permute-start | bytes 2600 | tf_op jit(solution)/shard_map/ppermute | solution.py:33
  (30 other events, 111.1 us)
Sparse Core Ops, SparseCore 0:
  71.7 27.2 reduce-scatter.4
  165.9 26.3 reduce-scatter.6
